TPU v7x, 32 devices: a whole 2x2x4 slice. The times are simulated.
32 devices in a mesh: ta: 8 (over z, y), col: 4 (over x, core).
Axes of the slice: x: 2, y: 2, z: 4, core: 2. Of those that a mesh axis runs over, the one named last changes fastest.
Arguments:
- strain: bfloat16 [2048, 512], P('col', 'ta'), may hold values from -6 to 6
- filter_taps: float32 [64], replicated, may hold values from -0.75 to 0.75
Outputs:
- cross_spectra: bfloat16 [4, 512, 128, 256], P('col', 'ta')
All inputs are finite; a program needn't handle non-finite values.
Results may differ from a plain program's by a relative error of at most 0.0066.
Values may be sent and summed in bfloat16 or wider, within the bound.
No kernel may reach another device: no remote copies, remote signals or barrier semaphores. Data moves between devices by JAX's collectives and lax.ppermute only.
A program may use at most 64 MiB of HBM per device.

v0:
```python
import jax
import jax.numpy as jnp
from jax import lax
from jax.sharding import PartitionSpec as P

NFFT = 256
NF = 128
LAGS = 128


def shifted(block, axis, distance):
    devices = range(lax.axis_size(axis))
    route = [((i - distance) % len(devices), i) for i in devices]
    return lax.ppermute(block, axis, route)


def from_behind(block, axis, distance):
    devices = range(lax.axis_size(axis))
    route = [(i - distance, i) for i in devices if i - distance in devices]
    return lax.ppermute(block, axis, route)


def tap_rows(filter_taps, outputs):
    tap_count = filter_taps.shape[0]
    window = 2 * outputs + tap_count
    flipped = filter_taps[::-1]
    period = jnp.concatenate([flipped, jnp.zeros((window + 2 - tap_count,), jnp.float32)])
    repeated = jnp.tile(period, outputs)[: outputs * window]
    return repeated.reshape(outputs, window)


def decimate(history, samples, filter_taps):
    channels, length = samples.shape
    tap_count = filter_taps.shape[0]
    outputs = min(length, NFFT) // 2
    blocks = length // (2 * outputs)
    joined = jnp.concatenate(
        [history, samples, jnp.zeros((channels, 2 * outputs - tap_count), jnp.float32)], axis=1
    )
    joined = joined.reshape(channels, blocks + 1, 2 * outputs)
    windows = jnp.concatenate([joined[:, :-1], joined[:, 1:, :tap_count]], axis=2)
    matrix = tap_rows(filter_taps, outputs)
    result = jnp.einsum("cbw,tw->cbt", windows, matrix, precision=lax.Precision.HIGHEST)
    return result.reshape(channels, blocks * outputs).astype(jnp.bfloat16)


def fourier_table():
    moment = lax.broadcasted_iota(jnp.int32, (NFFT, NF), 0)
    frequency = lax.broadcasted_iota(jnp.int32, (NFFT, NF), 1) + 1
    phase_index = moment * frequency % NFFT
    angles = phase_index.astype(jnp.float32) * (2.0 * jnp.pi / NFFT)
    window_taper = 0.5 - 0.5 * jnp.cos(moment.astype(jnp.float32) * (2.0 * jnp.pi / NFFT))
    return jnp.concatenate(
        [window_taper * jnp.cos(angles), -window_taper * jnp.sin(angles)], axis=1
    )


def whiten(filtered):
    channels, length = filtered.shape
    pieces = filtered.reshape(channels, length // NF, NF)
    segment_rows = jnp.concatenate([pieces[:, :-1], pieces[:, 1:]], axis=2)
    spectrum = jnp.einsum(
        "csn,nf->csf",
        segment_rows.astype(jnp.float32),
        fourier_table(),
        precision=lax.Precision.HIGHEST,
    )
    real_part = spectrum[..., :NF]
    imag_part = spectrum[..., NF:]
    powers = real_part * real_part + imag_part * imag_part
    mean_power = jnp.mean(powers, axis=-1, keepdims=True)
    whitening = 1.0 / jnp.sqrt(powers + mean_power + 1e-06)
    return jnp.concatenate([real_part * whitening, imag_part * whitening], axis=-1).astype(
        jnp.bfloat16
    )


def cross_block(own_rows, extended):
    rows, segments, columns = own_rows.shape
    own_pairs = own_rows.reshape(rows, 2 * segments, NF)
    turned = jnp.concatenate([-extended[..., NF:], extended[..., :NF]], axis=-1)
    far_pairs = jnp.stack(
        [extended.reshape(-1, 2 * segments, NF), turned.reshape(-1, 2 * segments, NF)], axis=2
    )
    step_rows = min(16, rows)
    reach = step_rows + LAGS
    results = []
    for first in range(0, rows, step_rows):
        own_part = own_pairs[first : first + step_rows]
        far_part = far_pairs[first : first + reach]
        combined = jnp.einsum(
            "cxf,dxof->cdof", own_part, far_part, preferred_element_type=jnp.float32
        )
        combined = combined.reshape(step_rows * reach, NFFT) / segments
        combined = jnp.concatenate([combined, jnp.zeros((step_rows, NFFT), jnp.float32)], axis=0)
        banded = combined.reshape(step_rows, reach + 1, NFFT)[:, :LAGS]
        results.append(banded.astype(jnp.bfloat16))
    return jnp.concatenate(results, axis=0)


def body(strain, filter_taps):
    tap_count = filter_taps.shape[0]
    regrouped = lax.all_to_all(strain, "ta", split_axis=0, concat_axis=1, tiled=True)
    filtered = decimate(
        jnp.zeros((regrouped.shape[0], tap_count), jnp.float32),
        regrouped.astype(jnp.float32),
        filter_taps,
    )
    whitened = whiten(filtered)
    block_rows, segments, columns = whitened.shape
    reach = LAGS // block_rows
    position = lax.axis_index("ta")
    extent = lax.axis_size("ta")
    pieces = []
    for offset in range(1, reach + 1):
        pieces.append(shifted(whitened, "ta", -offset))
    stacked = jnp.stack(pieces)
    beyond = from_behind(stacked, "col", -1)
    offsets_ahead = jnp.arange(1, reach + 1, dtype=jnp.int32).reshape(reach, 1, 1, 1)
    beyond_end = position + offsets_ahead >= extent
    chosen = jnp.where(beyond_end, beyond, stacked)
    ahead_rows = chosen.reshape(reach * block_rows, segments, columns)
    extended = jnp.concatenate([whitened, ahead_rows], axis=0)
    return cross_block(whitened, extended)[None]


def solution(mesh):
    return jax.shard_map(
        body,
        mesh=mesh,
        in_specs=(P("col", "ta"), P()),
        out_specs=P("col", "ta", None, None),
        check_vma=False,
    )
```

profile of v0, /device:TPU:1, one launch (start us, length us, event | category | flops | bytes accessed | tf_op | source)
XLA Modules:
  0.0 51.3 jit_solution(17561312377843437521)
XLA Ops:
  0.0 1.0 %copy.24 = bf16[512,64]{1,0:T(8,128)(2,1)S(1)} copy(bf16[512,64]{0,1:T(8,128)(2,1)} %param.2) | data formatting | bytes 131072 | tf_op args[0]
  1.0 0.8 %reshape.138 = bf16[8,2,2048]{2,1,0:T(2,128)(2,1)} reshape(bf16[8,64,64]{2,1,0:T(8,128)(2,1)S(1)} %bitcast.78) | data formatting | bytes 131072
  1.8 6.4 %all-to-all-start = ((bf16[8,2,2048]{2,1,0:T(2,128)(2,1)}), bf16[8,2,2048]{2,1,0:T(2,128)(2,1)S(1)}, u32[]{:S(2)}, u32[]{:S(2)}) async-start(bf16[8,2,2048]{2,1,0:T(2,128)(2,1)} %reshape.138), calls=%async_computation | async-start | bytes 131072 | tf_op jit(solution)/shard_map/all_to_all | solution.py:103
  8.2 0.5 %cosine_multiply_fusion = (f32[256,128]{1,0:T(8,128)S(1)}, f32[256,128]{1,0:T(8,128)S(1)}) fusion(s32[128]{0:T(128)S(1)} %iota_add_fusion, f32[256]{0:T(256)S(1)} %get-tuple-element.15, f32[256]{0:T(256)S(1)} %get-tuple-element.16), kind=kLoop, calls=%fused_computation.32 | loop fusion | flops 524288 | bytes 264704 | tf_op jit(solution)/shard_map/mul | solution.py:54
  8.7 0.7 %rev.3 = f32[64]{0:T(128)S(1)} reverse(f32[64]{0:T(128)} %param.3), dimensions={0} | reverse | bytes 512 | tf_op jit(solution)/shard_map/rev | solution.py:26
  9.6 0.2 tile.10
  10.0 3.9 %all-to-all-done = bf16[8,2,2048]{2,1,0:T(2,128)(2,1)S(1)} async-done(((bf16[8,2,2048]{2,1,0:T(2,128)(2,1)}), bf16[8,2,2048]{2,1,0:T(2,128)(2,1)S(1)}, u32[]{:S(2)}, u32[]{:S(2)}) %all-to-all-start) | async-done | bytes 65568 | tf_op jit(solution)/shard_map/all_to_all | solution.py:103
  13.9 0.1 reshape.139
  14.1 0.2 copy.25
  14.7 0.4 convolution_convert_fusion
  15.1 0.2 convolution_bitcast_fusion
  15.6 0.4 collective-permute-start.1
  16.0 1.1 %collective-permute-start = (bf16[64,1,256]{2,0,1:T(8,128)(2,1)S(1)}, bf16[64,1,256]{2,0,1:T(8,128)(2,1)S(1)}, u32[]{:S(2)}, u32[]{:S(2)}) collective-permute-start(bf16[64,1,256]{2,0,1:T(8,128)(2,1)S(1)} %maximum_convert_fusion), channel_id=1, source_target_pairs={{4,0},{8,4},{12,8},{16,12},{20,16},{24,20},{28,24},{0,28},{5,1},{9... | collective-permute-start | bytes 98312 | tf_op jit(solution)/shard_map/ppermute | solution.py:14
  17.2 1.3 %collective-permute-done.1 = bf16[64,1,256]{2,0,1:T(8,128)(2,1)S(1)} collective-permute-done((bf16[64,1,256]{2,0,1:T(8,128)(2,1)S(1)}, bf16[64,1,256]{2,0,1:T(8,128)(2,1)S(1)}, u32[]{:S(2)}, u32[]{:S(2)}) %collective-permute-start.1) | collective-permute-done | bytes 32800 | tf_op jit(solution)/shard_map/ppermute | solution.py:14
  18.4 0.4 collective-permute-done
  18.8 5.5 %collective-permute-start.2 = (bf16[2,64,1,256]{3,1,2,0:T(8,128)(2,1)S(1)}, bf16[2,64,1,256]{3,1,2,0:T(8,128)(2,1)S(1)}, u32[]{:S(2)}, u32[]{:S(2)}) collective-permute-start(bf16[2,64,1,256]{3,1,2,0:T(8,128)(2,1)S(1)} %pad_maximum_fusion.2), channel_id=1, source_target_pairs={{1,0},{2,1},{3,2},{5,4},{6,5},{7,6},{9,8},{10,9},{11,10},{13,12},{... | collective-permute-start | bytes 196616 | tf_op jit(solution)/shard_map/ppermute | solution.py:20
  24.4 0.1 copy.29
  24.6 0.8 %copy.42 = bf16[16,2,128,1]{0,1,3,2:T(2,128)(2,1)} copy(bf16[16,2,128,1]{2,1,0,3:T(2,128)(2,1)S(1)} %bitcast.86) | data formatting | bytes 16384 | tf_op jit(solution)/shard_map/slice | solution.py:89
  25.3 0.7 %copy.43 = bf16[16,2,128,1]{0,1,3,2:T(2,128)(2,1)} copy(bf16[16,2,128,1]{2,1,0,3:T(2,128)(2,1)S(1)} %bitcast.85) | data formatting | bytes 16384 | tf_op jit(solution)/shard_map/slice | solution.py:89
  26.1 0.1 copy.44
  26.2 0.8 %copy.41 = bf16[16,2,128,1]{0,1,3,2:T(2,128)(2,1)} copy(bf16[16,2,128,1]{2,1,0,3:T(2,128)(2,1)S(1)} %bitcast.83) | data formatting | bytes 16384 | tf_op jit(solution)/shard_map/slice | solution.py:89
  26.9 0.2 collective-permute-done.2
  27.4 0.1 copy.31
  27.5 0.1 copy.30
  27.7 0.4 pad_maximum_fusion
  28.0 0.9 %convert_bitcast_fusion = bf16[16,144,2,128]{1,0,2,3:T(8,128)(2,1)S(1)} fusion(bf16[16,2,128,1]{0,1,3,2:T(2,128)(2,1)S(1)} %copy.44, bf16[192,2,2,128]{0,1,2,3:T(2,128)(2,1)S(1)} %pad_maximum_fusion), kind=kOutput, calls=%fused_computation.1 | convolution fusion | flops 2949120 | bytes 1384448 | tf_op jit(solution)/shard_map/cxf,dxof->cdof/dot_general | solution.py:91
  28.9 2.5 %copy.39 = bf16[16,144,2,128]{3,2,1,0:T(2,128)(2,1)S(1)} copy(bf16[16,144,2,128]{1,0,2,3:T(8,128)(2,1)S(1)} %convert_bitcast_fusion) | data formatting | bytes 2359296 | tf_op jit(solution)/shard_map/cxf,dxof->cdof/transpose | solution.py:91
  31.4 0.2 copy.64
  31.7 0.4 reshape.131
  32.1 1.1 %slice.124 = bf16[16,128,256]{2,1,0:T(8,128)(2,1)} slice(bf16[16,145,256]{2,1,0:T(8,128)(2,1)S(1)} %reshape.131), slice={[0:16], [0:128], [0:256]} | slice | bytes 2097152 | tf_op jit(solution)/shard_map/slice | solution.py:96
  33.2 0.9 %convert_bitcast_fusion.1 = bf16[16,144,2,128]{1,0,2,3:T(8,128)(2,1)S(1)} fusion(bf16[16,2,128,1]{0,1,3,2:T(2,128)(2,1)S(1)} %copy-done.5, bf16[192,2,2,128]{0,1,2,3:T(2,128)(2,1)S(1)} %pad_maximum_fusion), kind=kOutput, calls=%fused_computation.2 | convolution fusion | flops 2949120 | bytes 1384448 | tf_op jit(solution)/shard_map/cxf,dxof->cdof/dot_general | solution.py:91
  34.1 2.5 %copy.37 = bf16[16,144,2,128]{3,2,1,0:T(2,128)(2,1)S(1)} copy(bf16[16,144,2,128]{1,0,2,3:T(8,128)(2,1)S(1)} %convert_bitcast_fusion.1) | data formatting | bytes 2359296 | tf_op jit(solution)/shard_map/cxf,dxof->cdof/transpose | solution.py:91
  36.5 0.2 copy.65
  36.8 0.4 reshape.129
  37.2 1.1 %slice.121 = bf16[16,128,256]{2,1,0:T(8,128)(2,1)} slice(bf16[16,145,256]{2,1,0:T(8,128)(2,1)S(1)} %reshape.129), slice={[0:16], [0:128], [0:256]} | slice | bytes 2097152 | tf_op jit(solution)/shard_map/slice | solution.py:96
  38.3 0.9 %convert_bitcast_fusion.2 = bf16[16,144,2,128]{1,0,2,3:T(8,128)(2,1)S(1)} fusion(bf16[16,2,128,1]{0,1,3,2:T(2,128)(2,1)S(1)} %copy-done.4, bf16[192,2,2,128]{0,1,2,3:T(2,128)(2,1)S(1)} %pad_maximum_fusion), kind=kOutput, calls=%fused_computation.3 | convolution fusion | flops 2949120 | bytes 1384448 | tf_op jit(solution)/shard_map/cxf,dxof->cdof/dot_general | solution.py:91
  39.2 2.5 %copy.35 = bf16[16,144,2,128]{3,2,1,0:T(2,128)(2,1)S(1)} copy(bf16[16,144,2,128]{1,0,2,3:T(8,128)(2,1)S(1)} %convert_bitcast_fusion.2) | data formatting | bytes 2359296 | tf_op jit(solution)/shard_map/cxf,dxof->cdof/transpose | solution.py:91
  41.7 0.2 copy.66
  41.9 0.4 reshape.127
  42.3 1.1 %slice.118 = bf16[16,128,256]{2,1,0:T(8,128)(2,1)} slice(bf16[16,145,256]{2,1,0:T(8,128)(2,1)S(1)} %reshape.127), slice={[0:16], [0:128], [0:256]} | slice | bytes 2097152 | tf_op jit(solution)/shard_map/slice | solution.py:96
  43.5 0.8 %convert_bitcast_fusion.3 = bf16[16,144,2,128]{1,0,2,3:T(8,128)(2,1)S(1)} fusion(bf16[16,2,128,1]{0,1,3,2:T(2,128)(2,1)S(1)} %copy-done.3, bf16[192,2,2,128]{0,1,2,3:T(2,128)(2,1)S(1)} %pad_maximum_fusion), kind=kOutput, calls=%fused_computation.4 | convolution fusion | flops 2949120 | bytes 1384448 | tf_op jit(solution)/shard_map/cxf,dxof->cdof/dot_general | solution.py:91
  44.2 2.5 %copy.33 = bf16[16,144,2,128]{3,2,1,0:T(2,128)(2,1)S(1)} copy(bf16[16,144,2,128]{1,0,2,3:T(8,128)(2,1)S(1)} %convert_bitcast_fusion.3) | data formatting | bytes 2359296 | tf_op jit(solution)/shard_map/cxf,dxof->cdof/transpose | solution.py:91
  46.7 0.2 copy.67
  47.0 0.4 reshape.125
  47.5 0.7 %copy-done = bf16[16,128,256]{2,1,0:T(8,128)(2,1)S(1)} copy-done((bf16[16,128,256]{2,1,0:T(8,128)(2,1)S(1)}, bf16[16,128,256]{2,1,0:T(8,128)(2,1)}, u32[]{:S(2)}) %copy-start) | copy-done | bytes 1048600
  48.2 0.5 %copy-done.1 = bf16[16,128,256]{2,1,0:T(8,128)(2,1)S(1)} copy-done((bf16[16,128,256]{2,1,0:T(8,128)(2,1)S(1)}, bf16[16,128,256]{2,1,0:T(8,128)(2,1)}, u32[]{:S(2)}) %copy-start.1) | copy-done | bytes 1048600
  48.7 0.3 copy-done.2
  49.0 2.3 %maximum_bitcast_fusion = bf16[1,64,128,256]{3,2,1,0:T(8,128)(2,1)} fusion(bf16[16,128,256]{2,1,0:T(8,128)(2,1)S(1)} %copy-done, bf16[16,128,256]{2,1,0:T(8,128)(2,1)S(1)} %copy-done.1, bf16[16,128,256]{2,1,0:T(8,128)(2,1)S(1)} %copy-done.2, bf16[16,128,256]{2,1,0:T(8,128)(2,1)S(1)} %slice.115), kind=kLoop, calls=%fused_computation | loop fusion | flops 6291456 | bytes 8388608 | tf_op jit(solution)/shard_map/broadcast_in_dim | solution.py:124
  (50 shorter events, 1.6 us)
Async XLA Ops:
  1.8 12.1 %all-to-all-start = ((bf16[8,2,2048]{2,1,0:T(2,128)(2,1)}), bf16[8,2,2048]{2,1,0:T(2,128)(2,1)S(1)}, u32[]{:S(2)}, u32[]{:S(2)}) async-start(bf16[8,2,2048]{2,1,0:T(2,128)(2,1)} %reshape.138), calls=%async_computation | async-start | bytes 131072 | tf_op jit(solution)/shard_map/all_to_all | solution.py:103
  15.6 2.8 %collective-permute-start.1 = (bf16[64,1,256]{2,0,1:T(8,128)(2,1)S(1)}, bf16[64,1,256]{2,0,1:T(8,128)(2,1)S(1)}, u32[]{:S(2)}, u32[]{:S(2)}) collective-permute-start(bf16[64,1,256]{2,0,1:T(8,128)(2,1)S(1)} %maximum_convert_fusion), channel_id=1, source_target_pairs={{8,0},{12,4},{16,8},{20,12},{24,16},{28,20},{0,24},{4,28},{9,1},{1... | collective-permute-start | bytes 98312 | tf_op jit(solution)/shard_map/ppermute | solution.py:14
  16.0 2.8 %collective-permute-start = (bf16[64,1,256]{2,0,1:T(8,128)(2,1)S(1)}, bf16[64,1,256]{2,0,1:T(8,128)(2,1)S(1)}, u32[]{:S(2)}, u32[]{:S(2)}) collective-permute-start(bf16[64,1,256]{2,0,1:T(8,128)(2,1)S(1)} %maximum_convert_fusion), channel_id=1, source_target_pairs={{4,0},{8,4},{12,8},{16,12},{20,16},{24,20},{28,24},{0,28},{5,1},{9... | collective-permute-start | bytes 98312 | tf_op jit(solution)/shard_map/ppermute | solution.py:14
  18.8 8.4 %collective-permute-start.2 = (bf16[2,64,1,256]{3,1,2,0:T(8,128)(2,1)S(1)}, bf16[2,64,1,256]{3,1,2,0:T(8,128)(2,1)S(1)}, u32[]{:S(2)}, u32[]{:S(2)}) collective-permute-start(bf16[2,64,1,256]{3,1,2,0:T(8,128)(2,1)S(1)} %pad_maximum_fusion.2), channel_id=1, source_target_pairs={{1,0},{2,1},{3,2},{5,4},{6,5},{7,6},{9,8},{10,9},{11,10},{13,12},{... | collective-permute-start | bytes 196616 | tf_op jit(solution)/shard_map/ppermute | solution.py:20
  32.1 1.1 %copy-start.5 = (bf16[16,2,128,1]{0,1,3,2:T(2,128)(2,1)S(1)}, bf16[16,2,128,1]{0,1,3,2:T(2,128)(2,1)}, u32[]{:S(2)}) copy-start(bf16[16,2,128,1]{0,1,3,2:T(2,128)(2,1)} %copy.43) | copy-start | bytes 24580
  37.2 1.1 %copy-start.4 = (bf16[16,2,128,1]{0,1,3,2:T(2,128)(2,1)S(1)}, bf16[16,2,128,1]{0,1,3,2:T(2,128)(2,1)}, u32[]{:S(2)}) copy-start(bf16[16,2,128,1]{0,1,3,2:T(2,128)(2,1)} %copy.42) | copy-start | bytes 24580
  41.9 1.6 %copy-start.3 = (bf16[16,2,128,1]{0,1,3,2:T(2,128)(2,1)S(1)}, bf16[16,2,128,1]{0,1,3,2:T(2,128)(2,1)}, u32[]{:S(2)}) copy-start(bf16[16,2,128,1]{0,1,3,2:T(2,128)(2,1)} %copy.41) | copy-start | bytes 24580
  46.9 1.2 %copy-start = (bf16[16,128,256]{2,1,0:T(8,128)(2,1)S(1)}, bf16[16,128,256]{2,1,0:T(8,128)(2,1)}, u32[]{:S(2)}) copy-start(bf16[16,128,256]{2,1,0:T(8,128)(2,1)} %slice.124) | copy-start | bytes 3145732
  47.4 1.3 %copy-start.1 = (bf16[16,128,256]{2,1,0:T(8,128)(2,1)S(1)}, bf16[16,128,256]{2,1,0:T(8,128)(2,1)}, u32[]{:S(2)}) copy-start(bf16[16,128,256]{2,1,0:T(8,128)(2,1)} %slice.121) | copy-start | bytes 3145732
  47.4 1.6 %copy-start.2 = (bf16[16,128,256]{2,1,0:T(8,128)(2,1)S(1)}, bf16[16,128,256]{2,1,0:T(8,128)(2,1)}, u32[]{:S(2)}) copy-start(bf16[16,128,256]{2,1,0:T(8,128)(2,1)} %slice.118) | copy-start | bytes 3145732
where the time goes:
time: 51.6 us; the launch traced here: 51.3 us
  local copies, waits for them, and re-layouts  23.8 us (46%)
  starting transfers between devices  13.5 us (26%)
  waiting for transfers between devices  5.81 us (11%)
  matrix products  4.04 us (8%)
  other arithmetic  3.7 us (7%)
    transpose x4, local copies, waits for them, and re-layouts, cross_block(): jnp.einsum('cxf,dxof->cdof', own_part, far_part, preferred_element_type=j...  9.84 us
    all_to_all x1, starting transfers between devices, body(): lax.all_to_all(strain, 'ta', split_axis=0, concat_axis=1, tiled=True)  6.38 us
    ppermute x1, starting transfers between devices, from_behind(): return lax.ppermute(block, axis, route)  5.55 us
    unnamed x21, local copies, waits for them, and re-layouts  4.04 us
    all_to_all x1, waiting for transfers between devices, body(): lax.all_to_all(strain, 'ta', split_axis=0, concat_axis=1, tiled=True)  3.94 us
    dot_general x4, matrix products, cross_block(): jnp.einsum('cxf,dxof->cdof', own_part, far_part, preferred_element_type=j...  3.4 us
    slice x4, local copies, waits for them, and re-layouts, cross_block(): banded = combined.reshape(step_rows, reach + 1, NFFT)[:, :LAGS]  3.38 us
    slice x9, local copies, waits for them, and re-layouts, cross_block(): own_part = own_pairs[first:first + step_rows]  2.43 us
  transfers between devices with their start and end apart: 4, of which 4 were waited for; matrix products, arithmetic and copies ran while one was open for 8% of the time, Pallas kernels for 0%

commit v1 on v0

--- a/solution.py
+++ b/solution.py
@@ -1,23 +1,15 @@
+import functools
+
 import jax
 import jax.numpy as jnp
 from jax import lax
+from jax.experimental import pallas as pl
+from jax.experimental.pallas import tpu as pltpu
 from jax.sharding import PartitionSpec as P
 
 NFFT = 256
 NF = 128
 LAGS = 128
-
-
-def shifted(block, axis, distance):
-    devices = range(lax.axis_size(axis))
-    route = [((i - distance) % len(devices), i) for i in devices]
-    return lax.ppermute(block, axis, route)
-
-
-def from_behind(block, axis, distance):
-    devices = range(lax.axis_size(axis))
-    route = [(i - distance, i) for i in devices if i - distance in devices]
-    return lax.ppermute(block, axis, route)
 
 
 def tap_rows(filter_taps, outputs):
@@ -75,32 +67,80 @@
     )
 
 
-def cross_block(own_rows, extended):
-    rows, segments, columns = own_rows.shape
-    own_pairs = own_rows.reshape(rows, 2 * segments, NF)
-    turned = jnp.concatenate([-extended[..., NF:], extended[..., :NF]], axis=-1)
-    far_pairs = jnp.stack(
-        [extended.reshape(-1, 2 * segments, NF), turned.reshape(-1, 2 * segments, NF)], axis=2
-    )
-    step_rows = min(16, rows)
-    reach = step_rows + LAGS
-    results = []
-    for first in range(0, rows, step_rows):
-        own_part = own_pairs[first : first + step_rows]
-        far_part = far_pairs[first : first + reach]
-        combined = jnp.einsum(
-            "cxf,dxof->cdof", own_part, far_part, preferred_element_type=jnp.float32
-        )
-        combined = combined.reshape(step_rows * reach, NFFT) / segments
-        combined = jnp.concatenate([combined, jnp.zeros((step_rows, NFFT), jnp.float32)], axis=0)
-        banded = combined.reshape(step_rows, reach + 1, NFFT)[:, :LAGS]
-        results.append(banded.astype(jnp.bfloat16))
-    return jnp.concatenate(results, axis=0)
+def gather_time(strain):
+    extent = lax.axis_size("ta")
+    if extent > 8:
+        return lax.all_to_all(strain, "ta", split_axis=0, concat_axis=1, tiled=True)
+    position = lax.axis_index("ta")
+    rows = strain.shape[0] // extent
+    blocks = strain.reshape(extent, rows, strain.shape[1])
+    received = [blocks[position]]
+    for distance in range(1, extent):
+        payload = blocks[(position + distance) % extent]
+        route = [(i, (i + distance) % extent) for i in range(extent)]
+        received.append(lax.ppermute(payload, "ta", route))
+    turned = jnp.stack([received[(-m) % extent] for m in range(extent)])
+    ordered = jnp.roll(turned, position, axis=0)
+    return ordered.transpose(1, 0, 2).reshape(rows, extent * strain.shape[1])
+
+
+def cross_kernel(segments, rows_per_step, own_ref, ext_ref, out_ref):
+    step = pl.program_id(0)
+    base = pl.multiple_of(step * rows_per_step, rows_per_step)
+    for i in range(rows_per_step):
+        c = base + i
+        acc_re = None
+        acc_im = None
+        for s in range(segments):
+            a = own_ref[s, pl.ds(c, 1), :]
+            window = ext_ref[s, pl.ds(base, LAGS + rows_per_step), :]
+            b = window[i : i + LAGS]
+            ar = a[:, :NF]
+            ai = a[:, NF:]
+            br = b[:, :NF]
+            bi = b[:, NF:]
+            t1 = ar * br
+            t2 = ai * bi
+            t3 = ai * br
+            t4 = ar * bi
+            if acc_re is None:
+                acc_re = [t1, t2]
+                acc_im = [t3, t4]
+            else:
+                acc_re = [acc_re[0] + t1, acc_re[1] + t2]
+                acc_im = [acc_im[0] + t3, acc_im[1] + t4]
+        re = (acc_re[0] + acc_re[1]) / segments
+        im = (acc_im[0] - acc_im[1]) / segments
+        out_ref[i, :, :NF] = re.astype(out_ref.dtype)
+        out_ref[i, :, NF:] = im.astype(out_ref.dtype)
+
+
+def cross_spectra(own, extended):
+    rows, segments, columns = own.shape
+    reach_rows = extended.shape[0]
+    own_t = own.astype(jnp.float32).transpose(1, 0, 2)
+    ext_t = extended.astype(jnp.float32).transpose(1, 0, 2)
+    rows_per_step = 8
+    return pl.pallas_call(
+        functools.partial(cross_kernel, segments, rows_per_step),
+        out_shape=jax.ShapeDtypeStruct((rows, LAGS, columns), jnp.bfloat16),
+        grid=(rows // rows_per_step,),
+        in_specs=[
+            pl.BlockSpec((segments, rows, columns), lambda i: (0, 0, 0)),
+            pl.BlockSpec((segments, reach_rows, columns), lambda i: (0, 0, 0)),
+        ],
+        out_specs=pl.BlockSpec((rows_per_step, LAGS, columns), lambda i: (i, 0, 0)),
+        cost_estimate=pl.CostEstimate(
+            flops=6 * rows * LAGS * NF * segments,
+            transcendentals=0,
+            bytes_accessed=rows * LAGS * columns * 2 + 4 * segments * (rows + reach_rows) * columns,
+        ),
+    )(own_t, ext_t)
 
 
 def body(strain, filter_taps):
     tap_count = filter_taps.shape[0]
-    regrouped = lax.all_to_all(strain, "ta", split_axis=0, concat_axis=1, tiled=True)
+    regrouped = gather_time(strain)
     filtered = decimate(
         jnp.zeros((regrouped.shape[0], tap_count), jnp.float32),
         regrouped.astype(jnp.float32),
@@ -109,19 +149,19 @@
     whitened = whiten(filtered)
     block_rows, segments, columns = whitened.shape
     reach = LAGS // block_rows
-    position = lax.axis_index("ta")
+    columns_n = lax.axis_size("col")
     extent = lax.axis_size("ta")
-    pieces = []
+    total = columns_n * extent
+
+    def linear(block):
+        return (block % extent) * columns_n + block // extent
+
+    pieces = [whitened]
     for offset in range(1, reach + 1):
-        pieces.append(shifted(whitened, "ta", -offset))
-    stacked = jnp.stack(pieces)
-    beyond = from_behind(stacked, "col", -1)
-    offsets_ahead = jnp.arange(1, reach + 1, dtype=jnp.int32).reshape(reach, 1, 1, 1)
-    beyond_end = position + offsets_ahead >= extent
-    chosen = jnp.where(beyond_end, beyond, stacked)
-    ahead_rows = chosen.reshape(reach * block_rows, segments, columns)
-    extended = jnp.concatenate([whitened, ahead_rows], axis=0)
-    return cross_block(whitened, extended)[None]
+        route = [(linear(b + offset), linear(b)) for b in range(total) if b + offset < total]
+        pieces.append(lax.ppermute(whitened, ("ta", "col"), route))
+    extended = jnp.concatenate(pieces, axis=0)
+    return cross_spectra(whitened, extended)[None]
 
 
 def solution(mesh):

time: 51.6 us -> 43.2 us (0.84)
  local copies, waits for them, and re-layouts: 23.8 us -> 2.79 us
  starting transfers between devices: 13.5 us -> 27.7 us
  Pallas kernels: 0 us -> 5.83 us
  matrix products: 4.04 us -> 0.63 us
  waiting for transfers between devices: 5.81 us -> 3.23 us
  other arithmetic: 3.7 us -> 2.25 us
    ppermute x3 -> x9, starting transfers between devices: 7.1 us -> 27.7 us  [the longest x2 15.1 us: body(): pieces.append(lax.ppermute(whitened, ('ta', 'col'), route))]
    transpose x4 -> x0, local copies, waits for them, and re-layouts: 9.84 us -> none  [cross_block(): jnp.einsum('cxf,dxof->cdof', own_part, far_part, preferred_element_type=j...]
    all_to_all x1 -> x0, starting transfers between devices: 6.38 us -> none  [body(): lax.all_to_all(strain, 'ta', split_axis=0, concat_axis=1, tiled=True)]
    pallas_call x0 -> x1, Pallas kernels: none -> 5.83 us  [cross_spectra(): pl.pallas_call(functools.partial(cross_kernel, segments, rows_per_step),...]
    slice x13 -> x0, local copies, waits for them, and re-layouts: 5.81 us -> none  [the longest x4 3.38 us: cross_block(): banded = combined.reshape(step_rows, reach + 1, NFFT)[:, :LAGS]]
    all_to_all x1 -> x0, waiting for transfers between devices: 3.94 us -> none  [body(): lax.all_to_all(strain, 'ta', split_axis=0, concat_axis=1, tiled=True)]
    dot_general x4 -> x0, matrix products: 3.4 us -> none  [cross_block(): jnp.einsum('cxf,dxof->cdof', own_part, far_part, preferred_element_type=j...]
    unnamed x21 -> x17, local copies, waits for them, and re-layouts: 4.04 us -> 1.1 us
  transfers between devices with their start and end apart: 4 -> 9, of which waited for: 4 -> 3; matrix products, arithmetic and copies ran while one was open for 8% -> 6% of each run, Pallas kernels for 0% -> 0%
where the time goes in v1:
time: 43.2 us; the launch traced here: 42.7 us
  starting transfers between devices  27.7 us (64%)
  Pallas kernels  5.83 us (13%)
  waiting for transfers between devices  3.23 us (7%)
  local copies, waits for them, and re-layouts  2.79 us (6%)
  other arithmetic  2.25 us (5%)
  matrix products  0.63 us (1%)
    ppermute x2, starting transfers between devices, body(): pieces.append(lax.ppermute(whitened, ('ta', 'col'), route))  15.1 us
    ppermute x7, starting transfers between devices, gather_time(): received.append(lax.ppermute(payload, 'ta', route))  12.5 us
    pallas_call x1, Pallas kernels, cross_spectra(): pl.pallas_call(functools.partial(cross_kernel, segments, rows_per_step),...  5.83 us
    ppermute x7, waiting for transfers between devices, gather_time(): received.append(lax.ppermute(payload, 'ta', route))  2.31 us
    unnamed x17, local copies, waits for them, and re-layouts  1.1 us
    ppermute x2, waiting for transfers between devices, body(): pieces.append(lax.ppermute(whitened, ('ta', 'col'), route))  0.93 us
  transfers between devices with their start and end apart: 9, of which 3 were waited for; matrix products, arithmetic and copies ran while one was open for 6% of the time, Pallas kernels for 0%

profile of v1, /device:TPU:1, one launch (start us, length us, event | category | flops | bytes accessed | tf_op | source)
XLA Modules:
  0.0 42.7 jit_solution(8906628615502523902)
XLA Ops:
  0.0 1.0 %copy.3 = bf16[512,64]{1,0:T(8,128)(2,1)S(1)} copy(bf16[512,64]{0,1:T(8,128)(2,1)} %param.2) | data formatting | bytes 131072 | tf_op args[0]
  1.0 2.1 %collective-permute-start.6 = (bf16[64,64]{1,0:T(8,128)(2,1)S(1)}, bf16[64,64]{1,0:T(8,128)(2,1)S(1)}, u32[]{:S(2)}, u32[]{:S(2)}) collective-permute-start(bf16[64,64]{1,0:T(8,128)(2,1)S(1)} %get-tuple-element.5), channel_id=1, source_target_pairs={{0,4},{4,8},{8,12},{12,16},{16,20},{20,24},{24,28},{28,0},{1,5},{5... | collective-permute-start | bytes 24584 | tf_op jit(solution)/shard_map/ppermute | solution.py:81
  3.2 1.3 %collective-permute-start.5 = (bf16[64,64]{1,0:T(8,128)(2,1)S(1)}, bf16[64,64]{1,0:T(8,128)(2,1)S(1)}, u32[]{:S(2)}, u32[]{:S(2)}) collective-permute-start(bf16[64,64]{1,0:T(8,128)(2,1)S(1)} %get-tuple-element.7), channel_id=1, source_target_pairs={{0,8},{4,12},{8,16},{12,20},{16,24},{20,28},{24,0},{28,4},{1,9},{5... | collective-permute-start | bytes 24584 | tf_op jit(solution)/shard_map/ppermute | solution.py:81
  4.5 2.3 %collective-permute-start.4 = (bf16[64,64]{1,0:T(8,128)(2,1)S(1)}, bf16[64,64]{1,0:T(8,128)(2,1)S(1)}, u32[]{:S(2)}, u32[]{:S(2)}) collective-permute-start(bf16[64,64]{1,0:T(8,128)(2,1)S(1)} %get-tuple-element.8), channel_id=1, source_target_pairs={{0,12},{4,16},{8,20},{12,24},{16,28},{20,0},{24,4},{28,8},{1,13},{... | collective-permute-start | bytes 24584 | tf_op jit(solution)/shard_map/ppermute | solution.py:81
  6.7 1.0 %collective-permute-start.3 = (bf16[64,64]{1,0:T(8,128)(2,1)S(1)}, bf16[64,64]{1,0:T(8,128)(2,1)S(1)}, u32[]{:S(2)}, u32[]{:S(2)}) collective-permute-start(bf16[64,64]{1,0:T(8,128)(2,1)S(1)} %get-tuple-element.9), channel_id=1, source_target_pairs={{0,16},{4,20},{8,24},{12,28},{16,0},{20,4},{24,8},{28,12},{1,17},{... | collective-permute-start | bytes 24584 | tf_op jit(solution)/shard_map/ppermute | solution.py:81
  7.7 2.1 %collective-permute-start = (bf16[64,64]{1,0:T(8,128)(2,1)S(1)}, bf16[64,64]{1,0:T(8,128)(2,1)S(1)}, u32[]{:S(2)}, u32[]{:S(2)}) collective-permute-start(bf16[64,64]{1,0:T(8,128)(2,1)S(1)} %get-tuple-element.12), channel_id=1, source_target_pairs={{0,28},{4,0},{8,4},{12,8},{16,12},{20,16},{24,20},{28,24},{1,29},{... | collective-permute-start | bytes 24584 | tf_op jit(solution)/shard_map/ppermute | solution.py:81
  9.8 0.5 %cosine_multiply_fusion = (f32[256,128]{1,0:T(8,128)S(1)}, f32[256,128]{1,0:T(8,128)S(1)}) fusion(s32[128]{0:T(128)S(1)} %iota_add_fusion, f32[256]{0:T(256)S(1)} %get-tuple-element.19, f32[256]{0:T(256)S(1)} %get-tuple-element.20), kind=kLoop, calls=%fused_computation.18 | loop fusion | flops 524288 | bytes 264704 | tf_op jit(solution)/shard_map/mul | solution.py:46
  10.4 0.7 %rev.3 = f32[64]{0:T(128)S(1)} reverse(f32[64]{0:T(128)} %param.3), dimensions={0} | reverse | bytes 512 | tf_op jit(solution)/shard_map/rev | solution.py:18
  11.1 0.1 pad.18.clone
  11.2 0.2 tile.10
  11.5 0.1 reshape.177
  11.6 0.0 collective-permute-done
  11.6 1.5 %collective-permute-start.1 = (bf16[64,64]{1,0:T(8,128)(2,1)S(1)}, bf16[64,64]{1,0:T(8,128)(2,1)S(1)}, u32[]{:S(2)}, u32[]{:S(2)}) collective-permute-start(bf16[64,64]{1,0:T(8,128)(2,1)S(1)} %get-tuple-element.11), channel_id=1, source_target_pairs={{0,24},{4,28},{8,0},{12,4},{16,8},{20,12},{24,16},{28,20},{1,25},{... | collective-permute-start | bytes 24584 | tf_op jit(solution)/shard_map/ppermute | solution.py:81
  13.1 1.1 %collective-permute-done.1 = bf16[64,64]{1,0:T(8,128)(2,1)S(1)} collective-permute-done((bf16[64,64]{1,0:T(8,128)(2,1)S(1)}, bf16[64,64]{1,0:T(8,128)(2,1)S(1)}, u32[]{:S(2)}, u32[]{:S(2)}) %collective-permute-start.1) | collective-permute-done | bytes 8224 | tf_op jit(solution)/shard_map/ppermute | solution.py:81
  14.2 2.3 %collective-permute-start.2 = (bf16[64,64]{1,0:T(8,128)(2,1)S(1)}, bf16[64,64]{1,0:T(8,128)(2,1)S(1)}, u32[]{:S(2)}, u32[]{:S(2)}) collective-permute-start(bf16[64,64]{1,0:T(8,128)(2,1)S(1)} %get-tuple-element.10), channel_id=1, source_target_pairs={{0,20},{4,24},{8,28},{12,0},{16,4},{20,8},{24,12},{28,16},{1,21},{... | collective-permute-start | bytes 24584 | tf_op jit(solution)/shard_map/ppermute | solution.py:81
  16.5 1.2 %collective-permute-done.2 = bf16[64,64]{1,0:T(8,128)(2,1)S(1)} collective-permute-done((bf16[64,64]{1,0:T(8,128)(2,1)S(1)}, bf16[64,64]{1,0:T(8,128)(2,1)S(1)}, u32[]{:S(2)}, u32[]{:S(2)}) %collective-permute-start.2) | collective-permute-done | bytes 8224 | tf_op jit(solution)/shard_map/ppermute | solution.py:81
  17.7 0.0 collective-permute-done.3
  17.7 0.0 collective-permute-done.4
  17.8 0.0 collective-permute-done.5
  17.8 0.0 collective-permute-done.6
  18.0 0.2 copy.4
  18.1 0.1 reshape.179
  18.2 0.1 maximum_maximum_fusion
  18.3 0.1 reshape.176
  18.6 0.4 convolution_convert_fusion
  19.0 0.2 convolution_bitcast_fusion
  19.3 0.1 fusion.19
  19.4 0.1 multiply_convert_fusion.1
  19.5 11.2 %collective-permute-start.8 = (bf16[64,1,256]{2,0,1:T(8,128)(2,1)S(1)}, bf16[64,1,256]{2,0,1:T(8,128)(2,1)S(1)}, u32[]{:S(2)}, u32[]{:S(2)}) collective-permute-start(bf16[64,1,256]{2,0,1:T(8,128)(2,1)S(1)} %pad_maximum_fusion), channel_id=1, source_target_pairs={{8,0},{12,4},{16,8},{20,12},{24,16},{28,20},{1,24},{5,28},{9,1},{1... | collective-permute-start | bytes 98312 | tf_op jit(solution)/shard_map/ppermute | solution.py:162
  30.7 3.9 %collective-permute-start.7 = (bf16[64,1,256]{2,0,1:T(8,128)(2,1)S(1)}, bf16[64,1,256]{2,0,1:T(8,128)(2,1)S(1)}, u32[]{:S(2)}, u32[]{:S(2)}) collective-permute-start(bf16[64,1,256]{2,0,1:T(8,128)(2,1)S(1)} %pad_maximum_fusion), channel_id=1, source_target_pairs={{4,0},{8,4},{12,8},{16,12},{20,16},{24,20},{28,24},{1,28},{5,1},{9... | collective-permute-start | bytes 98312 | tf_op jit(solution)/shard_map/ppermute | solution.py:162
  34.6 0.6 %maximum_convert_fusion.1.own_ref = f32[1,64,256]{2,1,0:T(8,128)} fusion(bf16[1,64,128]{2,1,0:T(8,128)(2,1)S(1)} %bitcast.59, bf16[1,64,128]{2,1,0:T(8,128)(2,1)S(1)} %bitcast.57), kind=kLoop, calls=%fused_computation.42 | loop fusion | flops 65536 | bytes 98304 | tf_op jit(solution)/shard_map/convert_element_type | solution.py:121
  35.3 0.0 collective-permute-done.8
  35.3 0.9 %collective-permute-done.7 = bf16[64,1,256]{2,0,1:T(8,128)(2,1)S(1)} collective-permute-done((bf16[64,1,256]{2,0,1:T(8,128)(2,1)S(1)}, bf16[64,1,256]{2,0,1:T(8,128)(2,1)S(1)}, u32[]{:S(2)}, u32[]{:S(2)}) %collective-permute-start.7) | collective-permute-done | bytes 32800 | tf_op jit(solution)/shard_map/ppermute | solution.py:162
  36.2 0.7 %maximum_convert_fusion.ext_ref = f32[1,192,256]{2,1,0:T(8,128)} fusion(bf16[1,64,256]{2,1,0:T(8,128)(2,1)S(1)} %bitcast.61, bf16[1,64,256]{2,1,0:T(8,128)(2,1)S(1)} %bitcast.62, bf16[1,64,256]{2,1,0:T(8,128)(2,1)S(1)} %maximum_bitcast_fusion.2), kind=kLoop, calls=%fused_computation.22 | loop fusion | flops 294912 | bytes 294912 | tf_op jit(solution)/shard_map/convert_element_type | solution.py:122
  36.9 5.8 %shard_map.28 = bf16[64,128,256]{2,1,0:T(8,128)(2,1)} custom-call(f32[1,64,256]{2,1,0:T(8,128)} %maximum_convert_fusion.1.own_ref, f32[1,192,256]{2,1,0:T(8,128)} %maximum_convert_fusion.ext_ref), custom_call_target="tpu_custom_call" | custom-call | flops 6291456 | bytes 4456448 | tf_op jit(solution)/shard_map/pallas_call | solution.py:124
  (33 shorter events, 0.4 us)
Async XLA Ops:
  1.0 16.8 %collective-permute-start.6 = (bf16[64,64]{1,0:T(8,128)(2,1)S(1)}, bf16[64,64]{1,0:T(8,128)(2,1)S(1)}, u32[]{:S(2)}, u32[]{:S(2)}) collective-permute-start(bf16[64,64]{1,0:T(8,128)(2,1)S(1)} %get-tuple-element.5), channel_id=1, source_target_pairs={{0,4},{4,8},{8,12},{12,16},{16,20},{20,24},{24,28},{28,0},{1,5},{5... | collective-permute-start | bytes 24584 | tf_op jit(solution)/shard_map/ppermute | solution.py:81
  3.2 14.6 %collective-permute-start.5 = (bf16[64,64]{1,0:T(8,128)(2,1)S(1)}, bf16[64,64]{1,0:T(8,128)(2,1)S(1)}, u32[]{:S(2)}, u32[]{:S(2)}) collective-permute-start(bf16[64,64]{1,0:T(8,128)(2,1)S(1)} %get-tuple-element.7), channel_id=1, source_target_pairs={{0,8},{4,12},{8,16},{12,20},{16,24},{20,28},{24,0},{28,4},{1,9},{5... | collective-permute-start | bytes 24584 | tf_op jit(solution)/shard_map/ppermute | solution.py:81
  4.5 13.3 %collective-permute-start.4 = (bf16[64,64]{1,0:T(8,128)(2,1)S(1)}, bf16[64,64]{1,0:T(8,128)(2,1)S(1)}, u32[]{:S(2)}, u32[]{:S(2)}) collective-permute-start(bf16[64,64]{1,0:T(8,128)(2,1)S(1)} %get-tuple-element.8), channel_id=1, source_target_pairs={{0,12},{4,16},{8,20},{12,24},{16,28},{20,0},{24,4},{28,8},{1,13},{... | collective-permute-start | bytes 24584 | tf_op jit(solution)/shard_map/ppermute | solution.py:81
  6.7 11.0 %collective-permute-start.3 = (bf16[64,64]{1,0:T(8,128)(2,1)S(1)}, bf16[64,64]{1,0:T(8,128)(2,1)S(1)}, u32[]{:S(2)}, u32[]{:S(2)}) collective-permute-start(bf16[64,64]{1,0:T(8,128)(2,1)S(1)} %get-tuple-element.9), channel_id=1, source_target_pairs={{0,16},{4,20},{8,24},{12,28},{16,0},{20,4},{24,8},{28,12},{1,17},{... | collective-permute-start | bytes 24584 | tf_op jit(solution)/shard_map/ppermute | solution.py:81
  7.7 3.9 %collective-permute-start = (bf16[64,64]{1,0:T(8,128)(2,1)S(1)}, bf16[64,64]{1,0:T(8,128)(2,1)S(1)}, u32[]{:S(2)}, u32[]{:S(2)}) collective-permute-start(bf16[64,64]{1,0:T(8,128)(2,1)S(1)} %get-tuple-element.12), channel_id=1, source_target_pairs={{0,28},{4,0},{8,4},{12,8},{16,12},{20,16},{24,20},{28,24},{1,29},{... | collective-permute-start | bytes 24584 | tf_op jit(solution)/shard_map/ppermute | solution.py:81
  11.6 2.6 %collective-permute-start.1 = (bf16[64,64]{1,0:T(8,128)(2,1)S(1)}, bf16[64,64]{1,0:T(8,128)(2,1)S(1)}, u32[]{:S(2)}, u32[]{:S(2)}) collective-permute-start(bf16[64,64]{1,0:T(8,128)(2,1)S(1)} %get-tuple-element.11), channel_id=1, source_target_pairs={{0,24},{4,28},{8,0},{12,4},{16,8},{20,12},{24,16},{28,20},{1,25},{... | collective-permute-start | bytes 24584 | tf_op jit(solution)/shard_map/ppermute | solution.py:81
  14.2 3.5 %collective-permute-start.2 = (bf16[64,64]{1,0:T(8,128)(2,1)S(1)}, bf16[64,64]{1,0:T(8,128)(2,1)S(1)}, u32[]{:S(2)}, u32[]{:S(2)}) collective-permute-start(bf16[64,64]{1,0:T(8,128)(2,1)S(1)} %get-tuple-element.10), channel_id=1, source_target_pairs={{0,20},{4,24},{8,28},{12,0},{16,4},{20,8},{24,12},{28,16},{1,21},{... | collective-permute-start | bytes 24584 | tf_op jit(solution)/shard_map/ppermute | solution.py:81
  19.5 15.8 %collective-permute-start.8 = (bf16[64,1,256]{2,0,1:T(8,128)(2,1)S(1)}, bf16[64,1,256]{2,0,1:T(8,128)(2,1)S(1)}, u32[]{:S(2)}, u32[]{:S(2)}) collective-permute-start(bf16[64,1,256]{2,0,1:T(8,128)(2,1)S(1)} %pad_maximum_fusion), channel_id=1, source_target_pairs={{8,0},{12,4},{16,8},{20,12},{24,16},{28,20},{1,24},{5,28},{9,1},{1... | collective-permute-start | bytes 98312 | tf_op jit(solution)/shard_map/ppermute | solution.py:162
  30.7 5.5 %collective-permute-start.7 = (bf16[64,1,256]{2,0,1:T(8,128)(2,1)S(1)}, bf16[64,1,256]{2,0,1:T(8,128)(2,1)S(1)}, u32[]{:S(2)}, u32[]{:S(2)}) collective-permute-start(bf16[64,1,256]{2,0,1:T(8,128)(2,1)S(1)} %pad_maximum_fusion), channel_id=1, source_target_pairs={{4,0},{8,4},{12,8},{16,12},{20,16},{24,20},{28,24},{1,28},{5,1},{9... | collective-permute-start | bytes 98312 | tf_op jit(solution)/shard_map/ppermute | solution.py:162
